TPU v7x, 256 devices: a whole 4x4x8 slice. The times are simulated.
256 devices in a mesh: row: 16 (over z, core), col: 16 (over y, x).
Axes of the slice: x: 4, y: 4, z: 8, core: 2. Of those that a mesh axis runs over, the one named last changes fastest.
Arguments:
- matrix: bfloat16 [4096, 262144], P('row', 'col'), may hold values from -60 to 60
- test_matrix: bfloat16 [262144, 512], P(('col', 'row')), may hold values from -0.0390625 to 0.0390625
Outputs:
- orthonormal: float32 [4096, 512], P(('row', 'col'))
- triangular: float32 [512, 512], replicated
All inputs are finite; a program needn't handle non-finite values.
Results may differ from a plain program's by a relative error of at most 0.0003.
Values may be sent and summed in bfloat16 or wider, within the bound.
No kernel may reach another device: no remote copies, remote signals or barrier semaphores. Data moves between devices by JAX's collectives and lax.ppermute only.
A program may use at most 128 MiB of HBM per device.

v0:
```python
import jax
import jax.numpy as jnp
from jax import lax
from jax.sharding import PartitionSpec as P


def probe_product(matrix, test_matrix):
    return jnp.dot(
        matrix,
        lax.all_gather(test_matrix, "row", axis=0, tiled=True),
        preferred_element_type=jnp.float32,
    )


def scatter_sum(value, axis, parts):
    pieces = value.reshape(parts, value.shape[0] // parts, *value.shape[1:])
    return lax.all_to_all(pieces, axis, 0, 0, tiled=False).sum(0)


def gather_rows(value, axis, parts):
    copies = jnp.broadcast_to(value[None], (parts, *value.shape))
    gathered = lax.all_to_all(copies, axis, 0, 0, tiled=False)
    return gathered.reshape(parts * value.shape[0], *value.shape[1:])


def shards(matrix, test_matrix):
    n_col = lax.axis_size("col")
    n_row = lax.axis_size("row")
    total_rows = matrix.shape[0] * n_row
    k = test_matrix.shape[1]
    partial_value = probe_product(matrix, test_matrix)
    own_rows = scatter_sum(partial_value, "col", n_col)
    sketch = gather_rows(own_rows, "col", n_col)
    width = k // n_col
    col = lax.axis_index("col")
    columns = lax.dynamic_slice_in_dim(sketch, col * width, width, 1)
    gram_part = jnp.dot(sketch.T, columns, precision=lax.Precision.HIGHEST)
    gram_part = gather_rows(scatter_sum(gram_part, "row", n_row), "row", n_row)
    blocks = gather_rows(gram_part.T, "col", n_col)
    gram = blocks.T / jnp.float32(total_rows)
    lower_factor = jnp.linalg.cholesky(gram)
    orthonormal = lax.linalg.triangular_solve(
        lower_factor, own_rows, left_side=False, lower=True, transpose_a=True
    )
    return (orthonormal, lower_factor.T)


def solution(mesh):
    in_specs = (P("row", "col"), P(("col", "row"), None))
    out_specs = (P(("row", "col"), None), P())
    return jax.shard_map(shards, mesh=mesh, in_specs=in_specs, out_specs=out_specs, check_vma=False)
```

profile of v0, /device:TPU:1, one launch (start us, length us, event | category | flops | bytes accessed | tf_op | source)
XLA Modules:
  0.0 345.5 jit_solution(3495870859918004758)
XLA Ops:
  7.2 0.7 all-gather.2.cloned.1.call-update
  7.9 101.5 %all-gather.2.cloned.1.call-done = bf16[16384,512]{1,0:T(8,128)(2,1)} async-done(((bf16[1024,512]{1,0:T(8,128)(2,1)}), bf16[16384,512]{1,0:T(8,128)(2,1)}) %all-gather.2.cloned.1.call-update) | async-done | bytes 16777232 | tf_op jit(solution)/shard_map/all_gather | solution.py:10
  109.4 10.5 %fusion.37 = f32[256,512]{1,0:T(8,128)S(1)} fusion(bf16[256,16384]{1,0:T(8,128)(2,1)} %param.2, bf16[16384,512]{1,0:T(8,128)(2,1)} %all-gather.2.cloned.1.call-done), kind=kOutput, calls=%fused_computation.74 | convolution fusion | flops 4294967296 | bytes 25690112 | tf_op jit(solution)/shard_map/dot_general | solution.py:8
  119.9 17.2 %all_to_all.25 = f32[16,16,512]{2,1,0:T(8,128)S(1)} all-to-all(f32[16,16,512]{2,1,0:T(8,128)S(1)} %bitcast.75), channel_id=1, replica_groups=mesh['row'=16,'col'=16] {'col'}, dimensions={0} | all-to-all | bytes 1048576 | tf_op jit(solution)/shard_map/all_to_all | solution.py:17
  137.1 0.9 broadcast_in_dim.7
  138.0 3.6 %all-to-all-start.1 = ((f32[16,16,512]{2,1,0:T(8,128)}), f32[16,16,512]{2,1,0:T(8,128)S(1)}, u32[]{:S(2)}, u32[]{:S(2)}) async-start(f32[16,16,512]{2,1,0:T(8,128)} %broadcast_in_dim.7), calls=%async_computation.1 | async-start | bytes 1048576 | tf_op jit(solution)/shard_map/all_to_all | solution.py:22
  141.5 10.1 %all-to-all-done.1 = f32[16,16,512]{2,1,0:T(8,128)S(1)} async-done(((f32[16,16,512]{2,1,0:T(8,128)}), f32[16,16,512]{2,1,0:T(8,128)S(1)}, u32[]{:S(2)}, u32[]{:S(2)}) %all-to-all-start.1) | async-done | bytes 524320 | tf_op jit(solution)/shard_map/all_to_all | solution.py:22
  151.8 0.7 fusion.11
  152.7 14.2 %all_to_all.26 = f32[16,1,1024]{2,1,0:T(1,128)S(1)} all-to-all(f32[16,1,1024]{2,1,0:T(1,128)S(1)} %reshape.80), channel_id=1, replica_groups=mesh['row'=16,'col'=16] {'row'}, dimensions={0} | all-to-all | bytes 131072 | tf_op jit(solution)/shard_map/all_to_all | solution.py:17
  166.9 0.5 broadcast.197
  167.4 0.8 reduce.24
  168.6 10.3 %all_to_all.27 = f32[16,1,1024]{2,1,0:T(1,128)S(1)} all-to-all(f32[16,1,1024]{2,1,0:T(1,128)S(1)} %reshape.82), channel_id=1, replica_groups=mesh['row'=16,'col'=16] {'row'}, dimensions={0} | all-to-all | bytes 131072 | tf_op jit(solution)/shard_map/all_to_all | solution.py:22
  178.9 0.8 reduce.25
  180.2 1.1 broadcast_in_dim.9
  181.3 3.8 %all-to-all-start.4 = ((f32[16,32,512]{2,1,0:T(8,128)}), f32[16,32,512]{2,1,0:T(8,128)S(1)}, u32[]{:S(2)}, u32[]{:S(2)}) async-start(f32[16,32,512]{2,1,0:T(8,128)} %broadcast_in_dim.9), calls=%async_computation.4 | async-start | bytes 2097152 | tf_op jit(solution)/shard_map/all_to_all | solution.py:22
  185.1 18.0 %all-to-all-done.4 = f32[16,32,512]{2,1,0:T(8,128)S(1)} async-done(((f32[16,32,512]{2,1,0:T(8,128)}), f32[16,32,512]{2,1,0:T(8,128)S(1)}, u32[]{:S(2)}, u32[]{:S(2)}) %all-to-all-start.4) | async-done | bytes 1048608 | tf_op jit(solution)/shard_map/all_to_all | solution.py:22
  203.1 0.3 copy.19
  203.4 0.2 fusion
  203.7 11.7 %cholesky.104 = f32[128,128]{1,0:T(8,128)S(1)} custom-call(f32[128,128]{1,0:T(8,128)S(1)} %cholesky.266), custom_call_target="Cholesky" | custom-call | tf_op jit(solution)/shard_map/jit(cholesky)/cholesky | solution.py:41
  215.6 9.8 %custom-call.30 = f32[1,128,128]{1,2,0:T(8,128)S(1)} custom-call(f32[1,128,128]{2,1,0:T(8,128)S(1)} %get-tuple-element.39), custom_call_target="InvertDiagBlocksLowerTriangular" | custom-call | tf_op jit(solution)/shard_map/jit(cholesky)/cholesky | solution.py:41
  225.4 0.3 constant_dynamic-update-slice_fusion.3
  225.7 0.3 convolution_subtract_fusion
  226.1 11.7 %cholesky.217 = f32[128,128]{1,0:T(8,128)S(1)} custom-call(f32[128,128]{1,0:T(8,128)S(1)} %cholesky.270), custom_call_target="Cholesky" | custom-call | tf_op jit(solution)/shard_map/jit(cholesky)/cholesky | solution.py:41
  237.8 10.0 %custom-call.31 = f32[1,128,128]{1,2,0:T(8,128)S(1)} custom-call(f32[1,128,128]{2,1,0:T(8,128)S(1)} %get-tuple-element.36), custom_call_target="InvertDiagBlocksLowerTriangular" | custom-call | tf_op jit(solution)/shard_map/jit(cholesky)/cholesky | solution.py:41
  247.8 0.3 convolution_dynamic-update-slice_fusion
  248.1 0.4 convolution_subtract_fusion.1
  248.5 11.7 %cholesky.238 = f32[128,128]{1,0:T(8,128)S(1)} custom-call(f32[128,128]{1,0:T(8,128)S(1)} %cholesky.275), custom_call_target="Cholesky" | custom-call | tf_op jit(solution)/shard_map/jit(cholesky)/cholesky | solution.py:41
  260.2 9.8 %custom-call.32 = f32[1,128,128]{1,2,0:T(8,128)S(1)} custom-call(f32[1,128,128]{2,1,0:T(8,128)S(1)} %get-tuple-element.33), custom_call_target="InvertDiagBlocksLowerTriangular" | custom-call | tf_op jit(solution)/shard_map/jit(cholesky)/cholesky | solution.py:41
  270.1 0.2 convolution_dynamic-update-slice_fusion.1
  270.3 0.4 convolution_subtract_fusion.2
  270.7 11.7 %cholesky.255 = f32[128,128]{1,0:T(8,128)S(1)} custom-call(f32[128,128]{1,0:T(8,128)S(1)} %convolution_subtract_fusion.2), custom_call_target="Cholesky" | custom-call | tf_op jit(solution)/shard_map/jit(cholesky)/cholesky | solution.py:41
  282.4 0.7 compare_reduce_fusion.1
  283.1 0.6 compare_reduce_fusion
  283.8 0.7 compare_reduce_fusion.2
  287.0 0.5 fusion.2
  287.5 8.5 %while.1 = (s32[]{:T(128)}, f32[512,512]{1,0:T(8,128)S(1)}, s32[4,2]{0,1:T(2,128)S(1)}, f32[4,128,128]{2,1,0:T(8,128)S(1)}, s32[]{:T(128)}) while((s32[]{:T(128)}, f32[512,512]{1,0:T(8,128)S(1)}, s32[4,2]{0,1:T(2,128)S(1)}, f32[4,128,128]{2,1,0:T(8,128)S(1)}, s32[]{:T(128)}) %tuple.36), condition=%wide.while_cond, body=%wide.while_body.sunk | while | flops 2 | bytes 131189 | solution.py:42
  287.6 0.6 fusion.47
  288.2 1.4 bitcast_dynamic-update-slice_fusion.2
  289.7 0.6 fusion.47
  290.3 1.4 bitcast_dynamic-update-slice_fusion.2
  291.8 0.6 fusion.47
  292.4 1.4 bitcast_dynamic-update-slice_fusion.2
  293.9 0.6 fusion.47
  294.5 1.4 bitcast_dynamic-update-slice_fusion.2
  296.0 39.3 %custom-call.33 = f32[4,128,128]{1,2,0:T(8,128)S(1)} custom-call(f32[4,128,128]{2,1,0:T(8,128)S(1)} %get-tuple-element.9), custom_call_target="InvertDiagBlocksLowerTriangular" | custom-call | tf_op jit(solution)/shard_map/triangular_solve | solution.py:42
  336.2 0.3 convolution_subtract_fusion.3
  336.7 0.6 pad_maximum_fusion
  337.4 1.3 copy.20
  (33 shorter events, 3.0 us)
Async XLA Ops:
  7.2 102.2 %all-gather.2.cloned.1.call-start = ((), (), s32[]{:S(2)}) async-start(), calls=%async_computation.5 | async-start | bytes 17825792 | tf_op jit(solution)/shard_map/all_gather | solution.py:10
  138.0 13.7 %all-to-all-start.1 = ((f32[16,16,512]{2,1,0:T(8,128)}), f32[16,16,512]{2,1,0:T(8,128)S(1)}, u32[]{:S(2)}, u32[]{:S(2)}) async-start(f32[16,16,512]{2,1,0:T(8,128)} %broadcast_in_dim.7), calls=%async_computation.1 | async-start | bytes 1048576 | tf_op jit(solution)/shard_map/all_to_all | solution.py:22
  181.3 21.8 %all-to-all-start.4 = ((f32[16,32,512]{2,1,0:T(8,128)}), f32[16,32,512]{2,1,0:T(8,128)S(1)}, u32[]{:S(2)}, u32[]{:S(2)}) async-start(f32[16,32,512]{2,1,0:T(8,128)} %broadcast_in_dim.9), calls=%async_computation.4 | async-start | bytes 2097152 | tf_op jit(solution)/shard_map/all_to_all | solution.py:22
Sparse Core Ops, SparseCore 0:
  9.8 99.5 all-gather.1
where the time goes:
time: 346 us
  waiting for transfers between devices  130 us (38%)
  other arithmetic  121 us (35%)
  blocking collectives  41.7 us (12%)
  between operations  16.8 us (5%)
  matrix products  14.5 us (4%)
  local copies, waits for them, and re-layouts  13.8 us (4%)
  starting transfers between devices  7.45 us (2%)
    all_gather x1, waiting for transfers between devices, probe_product(): lax.all_gather(test_matrix, 'row', axis=0, tiled=True)  101 us
    another operation x14, other arithmetic, shards(): lower_factor = jnp.linalg.cholesky(gram)  78.6 us
    another operation x3, other arithmetic, shards(): lax.linalg.triangular_solve(lower_factor, own_rows, left_side=False, lowe...  40 us
    all_to_all x2, blocking collectives, scatter_sum(): return lax.all_to_all(pieces, axis, 0, 0, tiled=False).sum(0)  31.4 us
    all_to_all x2, waiting for transfers between devices, gather_rows(): gathered = lax.all_to_all(copies, axis, 0, 0, tiled=False)  28.1 us
    dot_general x1, matrix products, probe_product(): jnp.dot(matrix, lax.all_gather(test_matrix, 'row', axis=0, tiled=True), p...  10.5 us
    all_to_all x1, blocking collectives, gather_rows(): gathered = lax.all_to_all(copies, axis, 0, 0, tiled=False)  10.3 us
    another operation x12, local copies, waits for them, and re-layouts  8.39 us
  transfers between devices with their start and end apart: 3, of which 3 were waited for; matrix products, arithmetic and copies ran while one was open for 0% of the time, Pallas kernels for 0%

commit v1 on v0

--- a/solution.py
+++ b/solution.py
@@ -7,7 +7,9 @@
 def probe_product(matrix, test_matrix):
     return jnp.dot(
         matrix,
-        lax.all_gather(test_matrix, "row", axis=0, tiled=True),
+        jnp.concatenate(
+            lax.all_to_all(jnp.stack([test_matrix] * lax.axis_size("row")), "row", 0, 0), axis=0
+        ),
         preferred_element_type=jnp.float32,
     )
 

time: 346 us -> 606 us (1.75)
  blocking collectives: 41.7 us -> 415 us
  waiting for transfers between devices: 130 us -> 28.9 us
  between operations: 16.8 us -> 3.44 us
    all_to_all x0 -> x1, blocking collectives: none -> 375 us  [probe_product(): lax.all_to_all(jnp.stack([test_matrix] * lax.axis_size('row')), 'row', 0, 0)]
    all_gather x1 -> x0, waiting for transfers between devices: 101 us -> none  [probe_product(): lax.all_gather(test_matrix, 'row', axis=0, tiled=True)]
  transfers between devices with their start and end apart: 3 -> 2, of which waited for: 3 -> 2; matrix products, arithmetic and copies ran while one was open for 0% -> 0% of each run, Pallas kernels for 0% -> 0%
where the time goes in v1:
time: 606 us; the launch traced here: 605 us
  blocking collectives  415 us (68%)
  other arithmetic  121 us (20%)
  waiting for transfers between devices  28.9 us (5%)
  local copies, waits for them, and re-layouts  17.4 us (3%)
  matrix products  11.4 us (2%)
  starting transfers between devices  7.41 us (1%)
    all_to_all x1, blocking collectives, probe_product(): lax.all_to_all(jnp.stack([test_matrix] * lax.axis_size('row')), 'row', 0, 0)  375 us
    another operation x14, other arithmetic, shards(): lower_factor = jnp.linalg.cholesky(gram)  78.6 us
    another operation x3, other arithmetic, shards(): lax.linalg.triangular_solve(lower_factor, own_rows, left_side=False, lowe...  40 us
    all_to_all x2, blocking collectives, scatter_sum(): return lax.all_to_all(pieces, axis, 0, 0, tiled=False).sum(0)  29.6 us
    all_to_all x2, waiting for transfers between devices, gather_rows(): gathered = lax.all_to_all(copies, axis, 0, 0, tiled=False)  28.9 us
  transfers between devices with their start and end apart: 2, of which 2 were waited for; matrix products, arithmetic and copies ran while one was open for 0% of the time, Pallas kernels for 0%

profile of v1, /device:TPU:1, one launch (start us, length us, event | category | flops | bytes accessed | tf_op | source)
XLA Modules:
  0.0 604.9 jit_solution(7362938672495359985)
XLA Ops:
  0.6 3.6 stack.2
  4.3 375.3 %all_to_all.30 = bf16[16,1024,512]{2,1,0:T(8,128)(2,1)S(1)} all-to-all(bf16[16,1024,512]{2,1,0:T(8,128)(2,1)S(1)} %stack.2), channel_id=1, replica_groups=mesh['row'=16,'col'=16] {'row'}, dimensions={0} | all-to-all | bytes 33554432 | tf_op jit(solution)/shard_map/all_to_all | solution.py:11
  379.5 7.4 %fusion.37 = f32[16,16,512]{2,1,0:T(8,128)S(1)} fusion(bf16[16,16,16384]{2,1,0:T(8,128)(2,1)} %bitcast.80, bf16[16384,512,1]{1,0,2:T(8,128)(2,1)S(1)} %bitcast.73), kind=kOutput, calls=%fused_computation.74 | convolution fusion | flops 4294967296 | bytes 25690112 | tf_op jit(solution)/shard_map/dot_general | solution.py:8
  386.9 17.9 %all_to_all.31 = f32[16,16,512]{2,1,0:T(8,128)S(1)} all-to-all(f32[16,16,512]{2,1,0:T(8,128)S(1)} %fusion.37), channel_id=1, replica_groups=mesh['row'=16,'col'=16] {'col'}, dimensions={0} | all-to-all | bytes 1048576 | tf_op jit(solution)/shard_map/all_to_all | solution.py:19
  404.9 0.9 broadcast_in_dim.7
  405.8 3.6 all-to-all-start.2
  409.4 11.0 %all-to-all-done.2 = f32[16,16,512]{2,1,0:T(8,128)S(1)} async-done(((f32[16,16,512]{2,1,0:T(8,128)}), f32[16,16,512]{2,1,0:T(8,128)S(1)}, u32[]{:S(2)}, u32[]{:S(2)}) %all-to-all-start.2) | async-done | bytes 524320 | tf_op jit(solution)/shard_map/all_to_all | solution.py:24
  420.5 0.7 fusion.11
  421.3 11.7 %all_to_all.32 = f32[16,1,1024]{2,1,0:T(1,128)S(1)} all-to-all(f32[16,1,1024]{2,1,0:T(1,128)S(1)} %reshape.85), channel_id=1, replica_groups=mesh['row'=16,'col'=16] {'row'}, dimensions={0} | all-to-all | bytes 131072 | tf_op jit(solution)/shard_map/all_to_all | solution.py:19
  433.1 0.5 broadcast.199
  433.6 0.8 reduce.24
  434.8 10.4 %all_to_all.33 = f32[16,1,1024]{2,1,0:T(1,128)S(1)} all-to-all(f32[16,1,1024]{2,1,0:T(1,128)S(1)} %reshape.87), channel_id=1, replica_groups=mesh['row'=16,'col'=16] {'row'}, dimensions={0} | all-to-all | bytes 131072 | tf_op jit(solution)/shard_map/all_to_all | solution.py:24
  445.2 0.8 reduce.25
  446.4 1.1 broadcast_in_dim.9
  447.5 3.8 all-to-all-start.5
  451.4 18.0 %all-to-all-done.5 = f32[16,32,512]{2,1,0:T(8,128)S(1)} async-done(((f32[16,32,512]{2,1,0:T(8,128)}), f32[16,32,512]{2,1,0:T(8,128)S(1)}, u32[]{:S(2)}, u32[]{:S(2)}) %all-to-all-start.5) | async-done | bytes 1048608 | tf_op jit(solution)/shard_map/all_to_all | solution.py:24
  469.4 0.3 copy.19
  469.7 0.2 fusion
  470.0 11.7 %cholesky.104 = f32[128,128]{1,0:T(8,128)S(1)} custom-call(f32[128,128]{1,0:T(8,128)S(1)} %cholesky.266), custom_call_target="Cholesky" | custom-call | tf_op jit(solution)/shard_map/jit(cholesky)/cholesky | solution.py:43
  481.8 9.8 %custom-call.30 = f32[1,128,128]{1,2,0:T(8,128)S(1)} custom-call(f32[1,128,128]{2,1,0:T(8,128)S(1)} %get-tuple-element.39), custom_call_target="InvertDiagBlocksLowerTriangular" | custom-call | tf_op jit(solution)/shard_map/jit(cholesky)/cholesky | solution.py:43
  491.7 0.3 constant_dynamic-update-slice_fusion.3
  492.0 0.3 convolution_subtract_fusion
  492.3 11.7 %cholesky.217 = f32[128,128]{1,0:T(8,128)S(1)} custom-call(f32[128,128]{1,0:T(8,128)S(1)} %cholesky.270), custom_call_target="Cholesky" | custom-call | tf_op jit(solution)/shard_map/jit(cholesky)/cholesky | solution.py:43
  504.1 10.0 %custom-call.31 = f32[1,128,128]{1,2,0:T(8,128)S(1)} custom-call(f32[1,128,128]{2,1,0:T(8,128)S(1)} %get-tuple-element.36), custom_call_target="InvertDiagBlocksLowerTriangular" | custom-call | tf_op jit(solution)/shard_map/jit(cholesky)/cholesky | solution.py:43
  514.1 0.3 convolution_dynamic-update-slice_fusion
  514.3 0.4 convolution_subtract_fusion.1
  514.7 11.7 %cholesky.238 = f32[128,128]{1,0:T(8,128)S(1)} custom-call(f32[128,128]{1,0:T(8,128)S(1)} %cholesky.275), custom_call_target="Cholesky" | custom-call | tf_op jit(solution)/shard_map/jit(cholesky)/cholesky | solution.py:43
  526.5 9.8 %custom-call.32 = f32[1,128,128]{1,2,0:T(8,128)S(1)} custom-call(f32[1,128,128]{2,1,0:T(8,128)S(1)} %get-tuple-element.33), custom_call_target="InvertDiagBlocksLowerTriangular" | custom-call | tf_op jit(solution)/shard_map/jit(cholesky)/cholesky | solution.py:43
  536.3 0.2 convolution_dynamic-update-slice_fusion.1
  536.5 0.4 convolution_subtract_fusion.2
  536.9 11.7 %cholesky.255 = f32[128,128]{1,0:T(8,128)S(1)} custom-call(f32[128,128]{1,0:T(8,128)S(1)} %convolution_subtract_fusion.2), custom_call_target="Cholesky" | custom-call | tf_op jit(solution)/shard_map/jit(cholesky)/cholesky | solution.py:43
  548.7 0.7 compare_reduce_fusion.1
  549.4 0.6 compare_reduce_fusion
  550.0 0.7 compare_reduce_fusion.2
  553.2 0.5 fusion.2
  553.7 8.5 %while.1 = (s32[]{:T(128)}, f32[512,512]{1,0:T(8,128)S(1)}, s32[4,2]{0,1:T(2,128)S(1)}, f32[4,128,128]{2,1,0:T(8,128)S(1)}, s32[]{:T(128)}) while((s32[]{:T(128)}, f32[512,512]{1,0:T(8,128)S(1)}, s32[4,2]{0,1:T(2,128)S(1)}, f32[4,128,128]{2,1,0:T(8,128)S(1)}, s32[]{:T(128)}) %tuple.36), condition=%wide.while_cond, body=%wide.while_body.sunk | while | flops 2 | bytes 131189 | solution.py:44
  553.8 0.6 fusion.47
  554.4 1.4 bitcast_dynamic-update-slice_fusion.2
  555.9 0.6 fusion.47
  556.5 1.4 bitcast_dynamic-update-slice_fusion.2
  558.1 0.6 fusion.47
  558.7 1.4 bitcast_dynamic-update-slice_fusion.2
  560.2 0.6 fusion.47
  560.8 1.4 bitcast_dynamic-update-slice_fusion.2
  562.2 39.3 %custom-call.33 = f32[4,128,128]{1,2,0:T(8,128)S(1)} custom-call(f32[4,128,128]{2,1,0:T(8,128)S(1)} %get-tuple-element.9), custom_call_target="InvertDiagBlocksLowerTriangular" | custom-call | tf_op jit(solution)/shard_map/triangular_solve | solution.py:44
  602.5 0.3 convolution_subtract_fusion.3
  603.0 0.6 pad_maximum_fusion
  603.6 1.3 copy.20
  (32 shorter events, 2.9 us)
Async XLA Ops:
  405.8 14.5 %all-to-all-start.2 = ((f32[16,16,512]{2,1,0:T(8,128)}), f32[16,16,512]{2,1,0:T(8,128)S(1)}, u32[]{:S(2)}, u32[]{:S(2)}) async-start(f32[16,16,512]{2,1,0:T(8,128)} %broadcast_in_dim.7), calls=%async_computation.2 | async-start | bytes 1048576 | tf_op jit(solution)/shard_map/all_to_all | solution.py:24
  447.5 21.8 %all-to-all-start.5 = ((f32[16,32,512]{2,1,0:T(8,128)}), f32[16,32,512]{2,1,0:T(8,128)S(1)}, u32[]{:S(2)}, u32[]{:S(2)}) async-start(f32[16,32,512]{2,1,0:T(8,128)} %broadcast_in_dim.9), calls=%async_computation.5 | async-start | bytes 2097152 | tf_op jit(solution)/shard_map/all_to_all | solution.py:24
